TPU v7x, 512 devices: a whole 4x8x8 slice. The times are simulated.
512 devices in a mesh: space: 64 (over z_lo, y, core), chan: 8 (over x, z_hi).
Axes of the slice: x: 4, y: 8, z: 8 (z_hi: 2, z_lo: 4; z = z_hi * 4 + z_lo), core: 2. Of those that a mesh axis runs over, the one named last changes fastest.
Arguments:
- features: bfloat16 [1, 128, 128, 2048], P(None, 'chan', 'space'), may hold values from -6 to 6
- top_map: int32 [64, 2048], P('space'), may hold values from 0 to 2048, as said below
- bottom_map: int32 [64, 2048], P('space'), may hold values from 0 to 2048, as said below
- first_weight: bfloat16 [128, 3, 3, 128], P('chan'), may hold values from -0.1875 to 0.1875
- first_bias: float32 [128], P('chan'), may hold values from -3 to 3
- second_weight: bfloat16 [256, 3, 3, 128], P('chan'), may hold values from -0.1875 to 0.1875
- second_bias: float32 [256], P('chan'), may hold values from -3 to 3
Outputs:
- hidden: bfloat16 [1, 128, 128, 2048], P(None, 'chan', 'space')
- coarse: bfloat16 [1, 256, 64, 1024], P(None, 'chan', 'space')
Inputs may be any that keep to these rules, and one draw needn't show every extreme that they name: `top_map`: each entry of row s, column k is k - 1, k or k + 1 taken modulo 2048, or 2048 for a missing neighbour at a face corner; exactly 4 entries of each row equal 2048. `bottom_map`: each entry of row s, column k is k - 1, k or k + 1 taken modulo 2048, or 2048 for a missing neighbour at a face corner; exactly 4 entries of each row equal 2048.
All inputs are finite; a program needn't handle non-finite values.
Results may differ from a plain program's by a relative error of at most 0.012.
Values may be sent and summed in bfloat16 or wider, within the bound.
No kernel may reach another device: no remote copies, remote signals or barrier semaphores. Data moves between devices by JAX's collectives and lax.ppermute only.
A program may use at most 64 MiB of HBM per device.

v0:
```python
import jax
import jax.numpy as jnp
from jax import lax
from jax.sharding import PartitionSpec as P


def shifted(array, axis, by):
    devices = lax.axis_size(axis)
    pairs = [(i, i + by) for i in range(devices) if 0 <= i + by < devices]
    return lax.ppermute(array, axis, pairs)


def remap_window(source, table, first_col, width):
    cycle = table.shape[0]
    cols = (first_col + jnp.arange(width)) % cycle
    picked = lax.dynamic_slice_in_dim(
        jnp.concatenate([table, table], axis=0), first_col % cycle, width, axis=0
    )
    same = source[..., 1 : width + 1]
    prev = source[..., 0:width]
    nxt = source[..., 2 : width + 2]
    zero = jnp.zeros_like(same)
    out = jnp.where(picked == (cols + cycle - 1) % cycle, prev, zero)
    out = jnp.where(picked == (cols + 1) % cycle, nxt, out)
    out = jnp.where(picked == cols, same, out)
    return out


def remap_full(row, table):
    cycle = table.shape[0]
    wrapped = jnp.concatenate([row[..., -1:], row, row[..., :1]], axis=-1)
    return remap_window(wrapped, table, 0, cycle)


def conv(x, w, stride):
    return lax.conv_general_dilated(
        x,
        w,
        window_strides=stride,
        padding="VALID",
        dimension_numbers=("NCHW", "OHWI", "NCHW"),
        preferred_element_type=jnp.float32,
    )


def per_device(features, top_map, bottom_map, first_weight, first_bias, second_weight, second_bias):
    groups = lax.axis_size("chan")
    me = lax.axis_index("chan")
    x = features[0]
    rows = x.shape[1]
    cycle = x.shape[2]
    block = cycle // groups
    upper_map = top_map[0]
    lower_map = bottom_map[0]
    w1 = lax.all_gather(first_weight, "chan", axis=0, tiled=True)
    b1 = lax.all_gather(first_bias, "chan", axis=0, tiled=True)
    w2 = lax.all_gather(second_weight, "chan", axis=0, tiled=True)
    b2 = lax.all_gather(second_bias, "chan", axis=0, tiled=True)
    above_src = shifted(x[:, rows - 1, :], "space", 1)
    below_src = shifted(x[:, 0, :], "space", -1)
    above = remap_full(above_src, upper_map)
    below = remap_full(below_src, lower_map)
    padded = jnp.concatenate([above[:, None], x, below[:, None]], axis=1)
    halo = 3
    width = block + 2 * halo
    ext = jnp.concatenate([padded[..., cycle - halo :], padded, padded[..., :halo]], axis=-1)
    sends = jnp.stack([ext[..., j * block : j * block + width] for j in range(groups)], 0)
    got = lax.all_to_all(sends, "chan", 0, 0, tiled=True)
    window = got.reshape((-1,) + got.shape[2:])
    pre1 = conv(window[None], w1, (1, 1))
    hidden_win = jax.nn.gelu(pre1 + b1[None, :, None, None]).astype(jnp.bfloat16)[0]
    hidden_out = lax.all_to_all(
        hidden_win[:, :, halo - 1 : halo - 1 + block], "chan", 0, 2, tiled=True
    )
    rim_src = shifted(hidden_win[:, rows - 1, :], "space", 1)
    rim = remap_window(rim_src, upper_map, me * block - 1, block + 2)
    stacked = jnp.concatenate([rim[:, None], hidden_win[:, :, 1 : block + 3]], axis=1)
    pre2 = conv(stacked[None], w2, (1, 2))
    coarse_win = jax.nn.gelu(pre2 + b2[None, :, None, None]).astype(jnp.bfloat16)[0]
    coarse_out = lax.all_to_all(coarse_win, "chan", 0, 2, tiled=True)
    return (hidden_out[None], coarse_out[None])


def solution(mesh):
    placed = (
        P(None, "chan", "space", None),
        P("space", None),
        P("space", None),
        P("chan", None, None, None),
        P("chan"),
        P("chan", None, None, None),
        P("chan"),
    )
    return jax.shard_map(
        per_device,
        mesh=mesh,
        in_specs=placed,
        out_specs=(P(None, "chan", "space", None), P(None, "chan", "space", None)),
        check_vma=False,
    )
```

profile of v0, /device:TPU:64, one launch (start us, length us, event | category | flops | bytes accessed | tf_op | source)
XLA Modules:
  0.0 199.2 jit_solution(16435346475391124692)
XLA Ops:
  0.6 0.9 copy.98
  1.6 1.9 collective-permute-start
  3.5 5.8 %collective-permute-start.1 = (bf16[16,2048]{1,0:T(8,128)(2,1)S(1)}, bf16[16,2048]{1,0:T(8,128)(2,1)S(1)}, u32[]{:S(2)}, u32[]{:S(2)}) collective-permute-start(bf16[16,2048]{1,0:T(8,128)(2,1)S(1)} %get-tuple-element.15), channel_id=1, source_target_pairs={{8,0},{16,8},{24,16},{32,24},{40,32},{48,40},{56,48},{64,56},{72,6... | collective-permute-start | bytes 196616 | tf_op jit(solution)/shard_map/ppermute | solution.py:10
  9.3 0.7 copy-done.4
  10.0 1.3 dynamic-slice
  14.3 34.2 %all-reduce.2 = (f32[128]{0:T(128)S(1)}, f32[256]{0:T(256)S(1)}) all-reduce(f32[128]{0:T(128)S(1)} %dynamic-update-slice, f32[256]{0:T(256)S(1)} %dynamic-update-slice.1), channel_id=1, replica_groups=mesh['space'=64,'chan'=8] {'chan'}, use_global_device_ids=true, to_apply=%add | all-reduce | flops 384 | bytes 3072
  48.9 0.7 fusion.64
  49.6 0.7 fusion.61
  50.3 0.7 fusion.60
  51.0 0.7 fusion.59
  51.7 0.7 fusion.58
  52.4 0.7 fusion.57
  53.1 0.7 fusion.56
  53.8 0.7 fusion.55
  54.6 3.6 %all-to-all-start = ((bf16[8,16,4,262]{3,1,2,0:T(8,128)(2,1)}), bf16[8,16,4,262]{3,1,2,0:T(8,128)(2,1)S(1)}, u32[]{:S(2)}, u32[]{:S(2)}) async-start(bf16[8,16,4,262]{3,1,2,0:T(8,128)(2,1)} %fusion.55), calls=%async_computation | async-start | bytes 786432 | tf_op jit(solution)/shard_map/all_to_all | solution.py:68
  58.2 49.5 %all_gather.12 = bf16[128,3,3,128]{3,0,2,1:T(8,128)(2,1)S(1)} all-gather(bf16[16,3,3,128]{3,0,2,1:T(8,128)(2,1)S(1)} %copy-done.2), channel_id=1, replica_groups=mesh['space'=64,'chan'=8] {'chan'}, dimensions={0}, use_global_device_ids=true | all-gather | bytes 331776 | tf_op jit(solution)/shard_map/all_gather | solution.py:55
  107.8 46.5 %all_gather.14 = bf16[256,3,3,128]{3,0,2,1:T(8,128)(2,1)S(1)} all-gather(bf16[32,3,3,128]{3,0,2,1:T(8,128)(2,1)S(1)} %copy-done.1), channel_id=1, replica_groups=mesh['space'=64,'chan'=8] {'chan'}, dimensions={0}, use_global_device_ids=true | all-gather | bytes 663552 | tf_op jit(solution)/shard_map/all_gather | solution.py:57
  154.7 0.7 copy-done.7
  156.4 1.9 collective-permute-start.2
  158.3 5.8 %collective-permute-done.2 = bf16[128,260]{0,1:T(8,128)(2,1)S(1)} collective-permute-done((bf16[128,260]{0,1:T(8,128)(2,1)S(1)}, bf16[128,260]{0,1:T(8,128)(2,1)S(1)}, u32[]{:S(2)}, u32[]{:S(2)}) %collective-permute-start.2) | collective-permute-done | bytes 66592 | tf_op jit(solution)/shard_map/ppermute | solution.py:10
  164.4 0.8 slice-done
  165.6 0.7 copy-done.8
  167.3 0.7 reduce
  168.1 0.7 reshape.47
  168.7 5.3 %all-to-all-start.2 = ((bf16[8,2,2048]{2,1,0:T(2,128)(2,1)}), bf16[8,2,2048]{2,1,0:T(2,128)(2,1)S(1)}, u32[]{:S(2)}, u32[]{:S(2)}) async-start(bf16[8,2,2048]{2,1,0:T(2,128)(2,1)} %reshape.47), calls=%async_computation.2 | async-start | bytes 131072 | tf_op jit(solution)/shard_map/all_to_all | solution.py:80
  174.1 0.9 slice-done.1
  175.0 0.8 copy.78
  175.8 8.8 %all-to-all-done.2 = bf16[8,2,2048]{2,1,0:T(2,128)(2,1)S(1)} async-done(((bf16[8,2,2048]{2,1,0:T(2,128)(2,1)}), bf16[8,2,2048]{2,1,0:T(2,128)(2,1)S(1)}, u32[]{:S(2)}, u32[]{:S(2)}) %all-to-all-start.2) | async-done | bytes 65568 | tf_op jit(solution)/shard_map/all_to_all | solution.py:80
  184.6 3.4 %all-to-all-start.1 = ((bf16[128,2,256]{2,1,0:T(2,128)(2,1)}), bf16[128,2,256]{2,1,0:T(2,128)(2,1)S(1)}, u32[]{:S(2)}, u32[]{:S(2)}) async-start(bf16[128,2,256]{2,1,0:T(2,128)(2,1)} %copy.78), calls=%async_computation.1 | async-start | bytes 262144 | tf_op jit(solution)/shard_map/all_to_all | solution.py:72
  188.1 0.7 broadcast_in_dim.67
  188.7 9.7 %all-to-all-done.1 = bf16[128,2,256]{2,1,0:T(2,128)(2,1)S(1)} async-done(((bf16[128,2,256]{2,1,0:T(2,128)(2,1)}), bf16[128,2,256]{2,1,0:T(2,128)(2,1)S(1)}, u32[]{:S(2)}, u32[]{:S(2)}) %all-to-all-start.1) | async-done | bytes 131104 | tf_op jit(solution)/shard_map/all_to_all | solution.py:72
  198.5 0.7 reshape.46
  (61 shorter events, 5.5 us)
Async XLA Ops:
  1.6 7.7 %copy-start.3 = (s32[1,2048]{1,0:T(1,128)S(1)}, s32[1,2048]{1,0:T(1,128)}, u32[]{:S(2)}) copy-start(s32[1,2048]{1,0:T(1,128)} %param.8) | copy-start | bytes 24580
  1.6 46.9 %collective-permute-start = (bf16[16,2048]{1,0:T(8,128)(2,1)S(1)}, bf16[16,2048]{1,0:T(8,128)(2,1)S(1)}, u32[]{:S(2)}, u32[]{:S(2)}) collective-permute-start(bf16[16,2048]{1,0:T(8,128)(2,1)S(1)} %get-tuple-element.14), channel_id=1, source_target_pairs={{0,8},{8,16},{16,24},{24,32},{32,40},{40,48},{48,56},{56,64},{64,7... | collective-permute-start | bytes 196616 | tf_op jit(solution)/shard_map/ppermute | solution.py:10
  3.5 45.0 %collective-permute-start.1 = (bf16[16,2048]{1,0:T(8,128)(2,1)S(1)}, bf16[16,2048]{1,0:T(8,128)(2,1)S(1)}, u32[]{:S(2)}, u32[]{:S(2)}) collective-permute-start(bf16[16,2048]{1,0:T(8,128)(2,1)S(1)} %get-tuple-element.15), channel_id=1, source_target_pairs={{8,0},{16,8},{24,16},{32,24},{40,32},{48,40},{56,48},{64,56},{72,6... | collective-permute-start | bytes 196616 | tf_op jit(solution)/shard_map/ppermute | solution.py:10
  9.3 0.7 copy-start.4
  12.6 0.7 copy-start.5
  13.5 0.7 copy-start.6
  54.5 3.7 %copy-start.2 = (bf16[16,3,3,128]{3,0,2,1:T(8,128)(2,1)S(1)}, bf16[16,3,3,128]{3,0,2,1:T(8,128)(2,1)}, u32[]{:S(2)}) copy-start(bf16[16,3,3,128]{3,0,2,1:T(8,128)(2,1)} %param.10) | copy-start | bytes 110596
  54.6 99.7 %all-to-all-start = ((bf16[8,16,4,262]{3,1,2,0:T(8,128)(2,1)}), bf16[8,16,4,262]{3,1,2,0:T(8,128)(2,1)S(1)}, u32[]{:S(2)}, u32[]{:S(2)}) async-start(bf16[8,16,4,262]{3,1,2,0:T(8,128)(2,1)} %fusion.55), calls=%async_computation | async-start | bytes 786432 | tf_op jit(solution)/shard_map/all_to_all | solution.py:68
  58.2 49.5 %copy-start.1 = (bf16[32,3,3,128]{3,0,2,1:T(8,128)(2,1)S(1)}, bf16[32,3,3,128]{3,0,2,1:T(8,128)(2,1)}, u32[]{:S(2)}) copy-start(bf16[32,3,3,128]{3,0,2,1:T(8,128)(2,1)} %param.12) | copy-start | bytes 221188
  154.7 0.7 copy-start.7
  156.2 2.1 %copy-start = (bf16[128,2,260]{0,1,2:T(2,128)(2,1)}, bf16[128,2,260]{0,1,2:T(2,128)(2,1)S(1)}, u32[]{:S(2)}) copy-start(bf16[128,2,260]{0,1,2:T(2,128)(2,1)S(1)} %slice_bitcast_fusion) | copy-start | bytes 399364
  156.4 7.7 %collective-permute-start.2 = (bf16[128,260]{0,1:T(8,128)(2,1)S(1)}, bf16[128,260]{0,1:T(8,128)(2,1)S(1)}, u32[]{:S(2)}, u32[]{:S(2)}) collective-permute-start(bf16[128,260]{0,1:T(8,128)(2,1)S(1)} %bitcast.104), channel_id=1, source_target_pairs={{0,8},{8,16},{16,24},{24,32},{32,40},{40,48},{48,56},{56,64},{64,7... | collective-permute-start | bytes 199688 | tf_op jit(solution)/shard_map/ppermute | solution.py:10
  164.3 0.9 slice-start
  165.6 0.7 copy-start.8
  168.7 15.8 %all-to-all-start.2 = ((bf16[8,2,2048]{2,1,0:T(2,128)(2,1)}), bf16[8,2,2048]{2,1,0:T(2,128)(2,1)S(1)}, u32[]{:S(2)}, u32[]{:S(2)}) async-start(bf16[8,2,2048]{2,1,0:T(2,128)(2,1)} %reshape.47), calls=%async_computation.2 | async-start | bytes 131072 | tf_op jit(solution)/shard_map/all_to_all | solution.py:80
  174.1 0.9 slice-start.1
  184.6 13.9 %all-to-all-start.1 = ((bf16[128,2,256]{2,1,0:T(2,128)(2,1)}), bf16[128,2,256]{2,1,0:T(2,128)(2,1)S(1)}, u32[]{:S(2)}, u32[]{:S(2)}) async-start(bf16[128,2,256]{2,1,0:T(2,128)(2,1)} %copy.78), calls=%async_computation.1 | async-start | bytes 262144 | tf_op jit(solution)/shard_map/all_to_all | solution.py:72
where the time goes:
time: 200 us; the launch traced here: 199 us
  blocking collectives  130 us (65%)
  waiting for transfers between devices  24.3 us (12%)
  starting transfers between devices  21.9 us (11%)
  local copies, waits for them, and re-layouts  16.6 us (8%)
  other arithmetic  2.91 us (1%)
  between operations  2.33 us (1%)
    all_gather x1, blocking collectives, per_device(): w1 = lax.all_gather(first_weight, 'chan', axis=0, tiled=True)  49.5 us
    all_gather x1, blocking collectives, per_device(): w2 = lax.all_gather(second_weight, 'chan', axis=0, tiled=True)  46.5 us
    unnamed x1, blocking collectives  34.2 us
    unnamed x38, local copies, waits for them, and re-layouts  11.9 us
    all_to_all x1, waiting for transfers between devices, per_device(): lax.all_to_all(hidden_win[:, :, halo - 1:halo - 1 + block], 'chan', 0, 2,...  9.74 us
    ppermute x3, starting transfers between devices, shifted(): return lax.ppermute(array, axis, pairs)  9.59 us
    all_to_all x1, waiting for transfers between devices, per_device(): coarse_out = lax.all_to_all(coarse_win, 'chan', 0, 2, tiled=True)  8.79 us
    ppermute x3, waiting for transfers between devices, shifted(): return lax.ppermute(array, axis, pairs)  5.76 us
  transfers between devices with their start and end apart: 6, of which 3 were waited for; matrix products, arithmetic and copies ran while one was open for 2% of the time, Pallas kernels for 0%

commit v1 on v0

--- a/solution.py
+++ b/solution.py
@@ -2,6 +2,11 @@
 import jax.numpy as jnp
 from jax import lax
 from jax.sharding import PartitionSpec as P
+
+
+def all_by_exchange(array, name, dim):
+    sent = jnp.stack([array] * lax.axis_size(name))
+    return jnp.concatenate(lax.all_to_all(sent, name, 0, 0), axis=dim)
 
 
 def shifted(array, axis, by):
@@ -52,7 +57,7 @@
     block = cycle // groups
     upper_map = top_map[0]
     lower_map = bottom_map[0]
-    w1 = lax.all_gather(first_weight, "chan", axis=0, tiled=True)
+    w1 = all_by_exchange(first_weight, "chan", 0)
     b1 = lax.all_gather(first_bias, "chan", axis=0, tiled=True)
     w2 = lax.all_gather(second_weight, "chan", axis=0, tiled=True)
     b2 = lax.all_gather(second_bias, "chan", axis=0, tiled=True)

time: 200 us -> 167 us (0.83)
  blocking collectives: 130 us -> 77.5 us
  starting transfers between devices: 21.9 us -> 37.7 us
  waiting for transfers between devices: 24.3 us -> 28.7 us
    all_gather x1 -> x0, blocking collectives: 49.5 us -> none  [per_device(): w1 = lax.all_gather(first_weight, 'chan', axis=0, tiled=True)]
    all_to_all x0 -> x1, starting transfers between devices: none -> 12 us  [all_by_exchange(): return jnp.concatenate(lax.all_to_all(sent, name, 0, 0), axis=dim)]
    all_to_all x0 -> x1, waiting for transfers between devices: none -> 4.6 us  [all_by_exchange(): return jnp.concatenate(lax.all_to_all(sent, name, 0, 0), axis=dim)]
    unnamed x1, blocking collectives: 34.2 us -> 31.8 us
    all_to_all x1, starting transfers between devices: 5.35 us -> 7.65 us  [per_device(): coarse_out = lax.all_to_all(coarse_win, 'chan', 0, 2, tiled=True)]
  transfers between devices with their start and end apart: 6 -> 7, of which waited for: 3 -> 4; matrix products, arithmetic and copies ran while one was open for 2% -> 6% of each run, Pallas kernels for 0% -> 0%
where the time goes in v1:
time: 167 us; the launch traced here: 166 us
  blocking collectives  77.5 us (46%)
  starting transfers between devices  37.7 us (23%)
  waiting for transfers between devices  28.7 us (17%)
  local copies, waits for them, and re-layouts  16.3 us (10%)
  other arithmetic  2.9 us (2%)
  between operations  2.35 us (1%)
    all_gather x1, blocking collectives, per_device(): w2 = lax.all_gather(second_weight, 'chan', axis=0, tiled=True)  45.7 us
    unnamed x1, blocking collectives  31.8 us
    all_to_all x1, starting transfers between devices, all_by_exchange(): return jnp.concatenate(lax.all_to_all(sent, name, 0, 0), axis=dim)  12 us
    unnamed x38, local copies, waits for them, and re-layouts  10.8 us
    all_to_all x1, waiting for transfers between devices, per_device(): lax.all_to_all(hidden_win[:, :, halo - 1:halo - 1 + block], 'chan', 0, 2,...  9.74 us
    ppermute x3, starting transfers between devices, shifted(): return lax.ppermute(array, axis, pairs)  9.59 us
    all_to_all x1, waiting for transfers between devices, per_device(): coarse_out = lax.all_to_all(coarse_win, 'chan', 0, 2, tiled=True)  8.56 us
    all_to_all x1, starting transfers between devices, per_device(): coarse_out = lax.all_to_all(coarse_win, 'chan', 0, 2, tiled=True)  7.65 us
  transfers between devices with their start and end apart: 7, of which 4 were waited for; matrix products, arithmetic and copies ran while one was open for 6% of the time, Pallas kernels for 0%

profile of v1, /device:TPU:64, one launch (start us, length us, event | category | flops | bytes accessed | tf_op | source)
XLA Modules:
  0.0 166.3 jit_solution(11377209908714645235)
XLA Ops:
  0.6 0.9 copy.100
  1.6 1.9 %collective-permute-start = (bf16[16,2048]{1,0:T(8,128)(2,1)S(1)}, bf16[16,2048]{1,0:T(8,128)(2,1)S(1)}, u32[]{:S(2)}, u32[]{:S(2)}) collective-permute-start(bf16[16,2048]{1,0:T(8,128)(2,1)S(1)} %get-tuple-element.14), channel_id=1, source_target_pairs={{0,8},{8,16},{16,24},{24,32},{32,40},{40,48},{48,56},{56,64},{64,7... | collective-permute-start | bytes 196616 | tf_op jit(solution)/shard_map/ppermute | solution.py:15
  3.5 5.8 %collective-permute-start.1 = (bf16[16,2048]{1,0:T(8,128)(2,1)S(1)}, bf16[16,2048]{1,0:T(8,128)(2,1)S(1)}, u32[]{:S(2)}, u32[]{:S(2)}) collective-permute-start(bf16[16,2048]{1,0:T(8,128)(2,1)S(1)} %get-tuple-element.15), channel_id=1, source_target_pairs={{8,0},{16,8},{24,16},{32,24},{40,32},{48,40},{56,48},{64,56},{72,6... | collective-permute-start | bytes 196616 | tf_op jit(solution)/shard_map/ppermute | solution.py:15
  9.3 0.8 stack.47
  10.1 12.0 %all-to-all-start.1 = ((bf16[8,16,3,3,128]{4,1,3,2,0:T(8,128)(2,1)}), bf16[8,16,3,3,128]{4,1,3,2,0:T(8,128)(2,1)S(1)}, u32[]{:S(2)}, u32[]{:S(2)}) async-start(bf16[8,16,3,3,128]{4,1,3,2,0:T(8,128)(2,1)} %stack.47), calls=%async_computation.1 | async-start | bytes 589824 | tf_op jit(solution)/shard_map/all_to_all | solution.py:9
  22.1 0.7 copy-done.4
  23.2 0.7 fusion.64
  23.9 0.7 fusion.61
  24.6 0.7 fusion.60
  25.3 0.7 fusion.59
  26.0 0.7 fusion.58
  26.7 0.7 fusion.57
  27.4 0.7 fusion.56
  28.1 0.7 fusion.55
  28.8 4.6 %all-to-all-done.1 = bf16[8,16,3,3,128]{4,1,3,2,0:T(8,128)(2,1)S(1)} async-done(((bf16[8,16,3,3,128]{4,1,3,2,0:T(8,128)(2,1)}), bf16[8,16,3,3,128]{4,1,3,2,0:T(8,128)(2,1)S(1)}, u32[]{:S(2)}, u32[]{:S(2)}) %all-to-all-start.1) | async-done | bytes 294944 | tf_op jit(solution)/shard_map/all_to_all | solution.py:9
  33.4 5.1 %all-to-all-start = ((bf16[8,16,4,262]{3,1,2,0:T(8,128)(2,1)}), bf16[8,16,4,262]{3,1,2,0:T(8,128)(2,1)S(1)}, u32[]{:S(2)}, u32[]{:S(2)}) async-start(bf16[8,16,4,262]{3,1,2,0:T(8,128)(2,1)} %fusion.55), calls=%async_computation | async-start | bytes 786432 | tf_op jit(solution)/shard_map/all_to_all | solution.py:73
  38.6 1.3 dynamic-slice
  41.7 31.8 %all-reduce.2 = (f32[128]{0:T(128)S(1)}, f32[256]{0:T(256)S(1)}) all-reduce(f32[128]{0:T(128)S(1)} %dynamic-update-slice, f32[256]{0:T(256)S(1)} %dynamic-update-slice.1), channel_id=1, replica_groups=mesh['space'=64,'chan'=8] {'chan'}, use_global_device_ids=true, to_apply=%add | all-reduce | flops 384 | bytes 3072
  73.6 45.7 %all_gather.10 = bf16[256,3,3,128]{3,0,2,1:T(8,128)(2,1)S(1)} all-gather(bf16[32,3,3,128]{3,0,2,1:T(8,128)(2,1)S(1)} %copy-done.1), channel_id=1, replica_groups=mesh['space'=64,'chan'=8] {'chan'}, dimensions={0}, use_global_device_ids=true | all-gather | bytes 663552 | tf_op jit(solution)/shard_map/all_gather | solution.py:62
  119.8 0.7 copy-done.7
  121.4 1.9 %collective-permute-start.2 = (bf16[128,260]{0,1:T(8,128)(2,1)S(1)}, bf16[128,260]{0,1:T(8,128)(2,1)S(1)}, u32[]{:S(2)}, u32[]{:S(2)}) collective-permute-start(bf16[128,260]{0,1:T(8,128)(2,1)S(1)} %bitcast.106), channel_id=1, source_target_pairs={{0,8},{8,16},{16,24},{24,32},{32,40},{40,48},{48,56},{56,64},{64,7... | collective-permute-start | bytes 199688 | tf_op jit(solution)/shard_map/ppermute | solution.py:15
  123.4 5.8 %collective-permute-done.2 = bf16[128,260]{0,1:T(8,128)(2,1)S(1)} collective-permute-done((bf16[128,260]{0,1:T(8,128)(2,1)S(1)}, bf16[128,260]{0,1:T(8,128)(2,1)S(1)}, u32[]{:S(2)}, u32[]{:S(2)}) %collective-permute-start.2) | collective-permute-done | bytes 66592 | tf_op jit(solution)/shard_map/ppermute | solution.py:15
  129.4 0.8 slice-done
  130.7 0.7 copy-done.8
  133.8 7.6 %all-to-all-start.3 = ((bf16[8,2,2048]{2,1,0:T(2,128)(2,1)}), bf16[8,2,2048]{2,1,0:T(2,128)(2,1)S(1)}, u32[]{:S(2)}, u32[]{:S(2)}) async-start(bf16[8,2,2048]{2,1,0:T(2,128)(2,1)} %reshape.53), calls=%async_computation.3 | async-start | bytes 131072 | tf_op jit(solution)/shard_map/all_to_all | solution.py:85
  141.4 0.9 slice-done.1
  142.3 0.8 copy.80
  143.1 8.6 %all-to-all-done.3 = bf16[8,2,2048]{2,1,0:T(2,128)(2,1)S(1)} async-done(((bf16[8,2,2048]{2,1,0:T(2,128)(2,1)}), bf16[8,2,2048]{2,1,0:T(2,128)(2,1)S(1)}, u32[]{:S(2)}, u32[]{:S(2)}) %all-to-all-start.3) | async-done | bytes 65568 | tf_op jit(solution)/shard_map/all_to_all | solution.py:85
  151.7 3.4 %all-to-all-start.2 = ((bf16[128,2,256]{2,1,0:T(2,128)(2,1)}), bf16[128,2,256]{2,1,0:T(2,128)(2,1)S(1)}, u32[]{:S(2)}, u32[]{:S(2)}) async-start(bf16[128,2,256]{2,1,0:T(2,128)(2,1)} %copy.80), calls=%async_computation.2 | async-start | bytes 262144 | tf_op jit(solution)/shard_map/all_to_all | solution.py:77
  155.2 0.7 broadcast_in_dim.67
  155.8 9.7 %all-to-all-done.2 = bf16[128,2,256]{2,1,0:T(2,128)(2,1)S(1)} async-done(((bf16[128,2,256]{2,1,0:T(2,128)(2,1)}), bf16[128,2,256]{2,1,0:T(2,128)(2,1)S(1)}, u32[]{:S(2)}, u32[]{:S(2)}) %all-to-all-start.2) | async-done | bytes 131104 | tf_op jit(solution)/shard_map/all_to_all | solution.py:77
  165.6 0.7 reshape.52
  (64 shorter events, 5.7 us)
Async XLA Ops:
  1.6 7.7 %copy-start.2 = (bf16[16,3,3,128]{3,0,2,1:T(8,128)(2,1)S(1)}, bf16[16,3,3,128]{3,0,2,1:T(8,128)(2,1)}, u32[]{:S(2)}) copy-start(bf16[16,3,3,128]{3,0,2,1:T(8,128)(2,1)} %param.10) | copy-start | bytes 110596
  1.6 21.1 %collective-permute-start = (bf16[16,2048]{1,0:T(8,128)(2,1)S(1)}, bf16[16,2048]{1,0:T(8,128)(2,1)S(1)}, u32[]{:S(2)}, u32[]{:S(2)}) collective-permute-start(bf16[16,2048]{1,0:T(8,128)(2,1)S(1)} %get-tuple-element.14), channel_id=1, source_target_pairs={{0,8},{8,16},{16,24},{24,32},{32,40},{40,48},{48,56},{56,64},{64,7... | collective-permute-start | bytes 196616 | tf_op jit(solution)/shard_map/ppermute | solution.py:15
  3.5 19.3 %collective-permute-start.1 = (bf16[16,2048]{1,0:T(8,128)(2,1)S(1)}, bf16[16,2048]{1,0:T(8,128)(2,1)S(1)}, u32[]{:S(2)}, u32[]{:S(2)}) collective-permute-start(bf16[16,2048]{1,0:T(8,128)(2,1)S(1)} %get-tuple-element.15), channel_id=1, source_target_pairs={{8,0},{16,8},{24,16},{32,24},{40,32},{48,40},{56,48},{64,56},{72,6... | collective-permute-start | bytes 196616 | tf_op jit(solution)/shard_map/ppermute | solution.py:15
  10.1 12.0 %copy-start.3 = (s32[1,2048]{1,0:T(1,128)S(1)}, s32[1,2048]{1,0:T(1,128)}, u32[]{:S(2)}) copy-start(s32[1,2048]{1,0:T(1,128)} %param.8) | copy-start | bytes 24580
  10.1 23.3 %all-to-all-start.1 = ((bf16[8,16,3,3,128]{4,1,3,2,0:T(8,128)(2,1)}), bf16[8,16,3,3,128]{4,1,3,2,0:T(8,128)(2,1)S(1)}, u32[]{:S(2)}, u32[]{:S(2)}) async-start(bf16[8,16,3,3,128]{4,1,3,2,0:T(8,128)(2,1)} %stack.47), calls=%async_computation.1 | async-start | bytes 589824 | tf_op jit(solution)/shard_map/all_to_all | solution.py:9
  22.0 0.7 copy-start.4
  33.4 7.8 %copy-start.5 = (f32[32]{0:T(128)S(1)}, f32[32]{0:T(128)}, u32[]{:S(2)}) copy-start(f32[32]{0:T(128)} %param.13) | copy-start | bytes 388
  33.4 8.0 %copy-start.6 = (f32[16]{0:T(128)S(1)}, f32[16]{0:T(128)}, u32[]{:S(2)}) copy-start(f32[16]{0:T(128)} %param.11) | copy-start | bytes 196
  33.4 85.9 %all-to-all-start = ((bf16[8,16,4,262]{3,1,2,0:T(8,128)(2,1)}), bf16[8,16,4,262]{3,1,2,0:T(8,128)(2,1)S(1)}, u32[]{:S(2)}, u32[]{:S(2)}) async-start(bf16[8,16,4,262]{3,1,2,0:T(8,128)(2,1)} %fusion.55), calls=%async_computation | async-start | bytes 786432 | tf_op jit(solution)/shard_map/all_to_all | solution.py:73
  38.6 35.1 %copy-start.1 = (bf16[32,3,3,128]{3,0,2,1:T(8,128)(2,1)S(1)}, bf16[32,3,3,128]{3,0,2,1:T(8,128)(2,1)}, u32[]{:S(2)}) copy-start(bf16[32,3,3,128]{3,0,2,1:T(8,128)(2,1)} %param.12) | copy-start | bytes 221188
  119.8 0.7 copy-start.7
  121.2 2.1 %copy-start = (bf16[128,2,260]{0,1,2:T(2,128)(2,1)}, bf16[128,2,260]{0,1,2:T(2,128)(2,1)S(1)}, u32[]{:S(2)}) copy-start(bf16[128,2,260]{0,1,2:T(2,128)(2,1)S(1)} %slice_bitcast_fusion) | copy-start | bytes 399364
  121.4 7.7 %collective-permute-start.2 = (bf16[128,260]{0,1:T(8,128)(2,1)S(1)}, bf16[128,260]{0,1:T(8,128)(2,1)S(1)}, u32[]{:S(2)}, u32[]{:S(2)}) collective-permute-start(bf16[128,260]{0,1:T(8,128)(2,1)S(1)} %bitcast.106), channel_id=1, source_target_pairs={{0,8},{8,16},{16,24},{24,32},{32,40},{40,48},{48,56},{56,64},{64,7... | collective-permute-start | bytes 199688 | tf_op jit(solution)/shard_map/ppermute | solution.py:15
  129.3 0.9 slice-start
  130.6 0.7 copy-start.8
  133.8 17.9 %all-to-all-start.3 = ((bf16[8,2,2048]{2,1,0:T(2,128)(2,1)}), bf16[8,2,2048]{2,1,0:T(2,128)(2,1)S(1)}, u32[]{:S(2)}, u32[]{:S(2)}) async-start(bf16[8,2,2048]{2,1,0:T(2,128)(2,1)} %reshape.53), calls=%async_computation.3 | async-start | bytes 131072 | tf_op jit(solution)/shard_map/all_to_all | solution.py:85
  141.4 0.9 slice-start.1
  151.7 13.9 %all-to-all-start.2 = ((bf16[128,2,256]{2,1,0:T(2,128)(2,1)}), bf16[128,2,256]{2,1,0:T(2,128)(2,1)S(1)}, u32[]{:S(2)}, u32[]{:S(2)}) async-start(bf16[128,2,256]{2,1,0:T(2,128)(2,1)} %copy.80), calls=%async_computation.2 | async-start | bytes 262144 | tf_op jit(solution)/shard_map/all_to_all | solution.py:77
